TPU v7x, 256 devices: a whole 4x4x8 slice. The times are simulated.
256 devices in a mesh: sub: 64 (over z, x, core), harm: 4 (over y).
Axes of the slice: x: 4, y: 4, z: 8, core: 2. Of those that a mesh axis runs over, the one named last changes fastest.
Arguments:
- right_side: float32 [16, 128, 16384], P(None, None, 'sub'), may hold values from -6 to 6
- border_side: float32 [16, 128, 2048], P(None, None, 'sub'), may hold values from -6 to 6
- precond_tiles: bfloat16 [32768, 128, 128], P('sub', 'harm'), may hold values from -0.375 to 0.375
- tile_out: int32 [32768], P('sub'), may hold values from 0 to 255
- tile_in: int32 [32768], P('sub'), may hold values from 0 to 255
- couple_tiles: bfloat16 [16384, 128, 128], P('sub', 'harm'), may hold values from -0.1875 to 0.1875
- return_tiles: bfloat16 [16384, 128, 128], P('sub', 'harm'), may hold values from -0.5 to 0.5
- couple_node: int32 [16384], P('sub'), may hold values from 0 to 255
- border_owner: int32 [16384, 1], P('sub'), may hold values from 0 to 63; in each aligned block of 256 rows (0 to 255, 256 to 511, ...) at most 8 rows name the same one
- border_row: int32 [16384], P('sub'), may hold values from 0 to 31
- border_inverse: bfloat16 [2048, 128, 128], P('sub', 'harm'), may hold values from -0.5 to 0.5
Outputs:
- interior_update: float32 [16, 128, 16384], P(None, 'harm', 'sub')
- border_update: float32 [16, 128, 2048], P(None, 'harm', 'sub')
Inputs may be any that keep to these rules, and one draw needn't show every extreme that they name: `border_owner`: among the rows of one subcircuit at most 8 name one owner, a bound that some block reaches of them.
All inputs are finite; a program needn't handle non-finite values.
Results may differ from a plain program's by a relative error of at most 0.005.
Values may be sent and summed in bfloat16 or wider, within the bound.
No kernel may reach another device: no remote copies, remote signals or barrier semaphores. Data moves between devices by JAX's collectives and lax.ppermute only.
A program may use at most 128 MiB of HBM per device.

v0:
```python
import jax
import jax.numpy as jnp
from jax import lax
from jax.sharding import PartitionSpec as P


def collect(values, targets, row_total, first_row=0):
    marks = (
        first_row + jnp.arange(row_total, dtype=jnp.int32)[:, None] == targets[None, :]
    ).astype(jnp.float32)
    flat_rows = values.reshape(values.shape[0], -1)
    summed = jnp.dot(
        marks, flat_rows, precision=lax.Precision.HIGHEST, preferred_element_type=jnp.float32
    )
    return summed.reshape((row_total,) + values.shape[1:])


def tile_product(tile_set, columns, targets, segment_total):
    product = jnp.einsum("tok,trk->tro", tile_set, columns, preferred_element_type=jnp.float32)
    return collect(product, targets, segment_total)


def on_device(
    right_side,
    border_side,
    precond_tiles,
    tile_out,
    tile_in,
    couple_tiles,
    return_tiles,
    couple_node,
    border_owner,
    border_row,
    border_inverse,
):
    harm_block = precond_tiles.shape[1]
    node_count = right_side.shape[2]
    row_count = border_side.shape[2]
    touch_count = couple_node.shape[0]
    sub_count = lax.axis_size("sub")
    harm_offset = lax.axis_index("harm") * harm_block
    side_nodes = jnp.transpose(right_side, (2, 0, 1))
    border_nodes = jnp.transpose(border_side, (2, 0, 1))
    own_border = lax.dynamic_slice_in_dim(border_nodes, harm_offset, harm_block, 2)
    own_side = lax.dynamic_slice_in_dim(side_nodes, harm_offset, harm_block, 2)
    side_low = side_nodes.astype(jnp.bfloat16)
    first_pass = tile_product(precond_tiles, side_low[tile_in], tile_out, node_count).astype(
        jnp.bfloat16
    )
    first_full = lax.all_gather(first_pass, "harm", axis=2, tiled=True)
    partials = jnp.einsum(
        "tok,trk->tro", couple_tiles, first_full[couple_node], preferred_element_type=jnp.float32
    )
    owner_list = border_owner[:, 0]
    value_shape = partials.shape[1:]
    capacity = min(touch_count, max(4, 2 * touch_count // sub_count))
    owner_marks = (owner_list[:, None] == jnp.arange(sub_count, dtype=jnp.int32)[None, :]).astype(
        jnp.int32
    )
    earlier = jnp.cumsum(owner_marks, axis=0) - owner_marks
    slot_index = owner_list * capacity + jnp.sum(earlier * owner_marks, axis=1)
    slot_place = jnp.arange(sub_count * capacity, dtype=jnp.int32)[:, None] == slot_index[None, :]
    place_float = slot_place.astype(jnp.float32)
    send_values = jnp.dot(
        place_float,
        partials.reshape(touch_count, -1),
        precision=lax.Precision.HIGHEST,
        preferred_element_type=jnp.float32,
    )
    send_rows = jnp.sum(slot_place.astype(jnp.int32) * border_row[None, :], axis=1)
    send_values = send_values.reshape((sub_count, capacity) + value_shape)
    send_rows = send_rows.reshape((sub_count, capacity))
    arrived, arrived_rows = (
        lax.all_to_all(send_values, "sub", split_axis=0, concat_axis=0, tiled=True),
        lax.all_to_all(send_rows, "sub", split_axis=0, concat_axis=0, tiled=True),
    )
    incoming = collect(
        arrived.reshape((sub_count * capacity,) + value_shape), arrived_rows.reshape(-1), row_count
    )
    residual_low = (own_border - incoming).astype(jnp.bfloat16)
    residual_full = lax.all_gather(residual_low, "harm", axis=2, tiled=True)
    solved = jnp.einsum(
        "bok,brk->bro", border_inverse, residual_full, preferred_element_type=jnp.float32
    )
    solved, solved_low = (solved, solved.astype(jnp.bfloat16))
    replies = solved_low[arrived_rows]
    returned = lax.all_to_all(replies, "sub", split_axis=0, concat_axis=0, tiled=True)
    returned_flat = returned.reshape(sub_count * capacity, -1)
    touch_low = jnp.dot(
        slot_place.astype(jnp.bfloat16).T, returned_flat, preferred_element_type=jnp.float32
    )
    touch_low = touch_low.astype(jnp.bfloat16).reshape((touch_count,) + value_shape)
    touch_full = lax.all_gather(touch_low, "harm", axis=2, tiled=True)
    correction = tile_product(return_tiles, touch_full, couple_node, node_count)
    update_low = (own_side - correction).astype(jnp.bfloat16)
    update_full = lax.all_gather(update_low, "harm", axis=2, tiled=True)
    second_pass = tile_product(precond_tiles, update_full[tile_in], tile_out, node_count)
    return (jnp.transpose(second_pass, (1, 2, 0)), jnp.transpose(solved, (1, 2, 0)))


def solution(mesh):
    in_specs = (
        P(None, None, "sub"),
        P(None, None, "sub"),
        P("sub", "harm", None),
        P("sub"),
        P("sub"),
        P("sub", "harm", None),
        P("sub", "harm", None),
        P("sub"),
        P("sub", None),
        P("sub"),
        P("sub", "harm", None),
    )
    out_specs = (P(None, "harm", "sub"), P(None, "harm", "sub"))
    return jax.shard_map(
        on_device, mesh=mesh, in_specs=in_specs, out_specs=out_specs, check_vma=False
    )
```

profile of v0, /device:TPU:2, one launch (start us, length us, event | category | flops | bytes accessed | tf_op | source)
XLA Modules:
  0.0 258.4 jit_solution(11936853341196245962)
XLA Ops:
  8.1 2.2 copy.72
  10.3 2.7 %gather_fusion = bf16[512,16,128]{2,1,0:T(8,128)(2,1)} fusion(bf16[256,16,128]{2,1,0:T(8,128)(2,1)S(1)} %bitcast.106, s32[1024]{0:T(1024)S(1)} %pad_clamp_fusion.2), kind=kCustom, calls=%fused_computation | custom fusion | bytes 4196352 | tf_op jit(solution)/shard_map/gather | solution.py:47
  13.0 7.1 %fusion.34 = f32[512,16,32]{2,1,0:T(8,128)} fusion(bf16[512,16,128]{2,1,0:T(8,128)(2,1)} %gather_fusion, bf16[512,32,128]{2,1,0:T(8,128)(2,1)} %param.13), kind=kOutput, calls=%fused_computation.53 | convolution fusion | flops 67108864 | bytes 7340032 | tf_op jit(solution)/shard_map/tok,trk->tro/dot_general | solution.py:19
  20.1 2.8 %copy.73 = f32[512,16,32]{0,2,1:T(8,128)S(1)} copy(f32[512,16,32]{2,1,0:T(8,128)} %fusion.34) | data formatting | bytes 2097152 | tf_op jit(solution)/shard_map/tok,trk->tro/dot_general | solution.py:19
  26.4 12.0 %all-to-all-start = ((s32[64,1,8]{2,1,0:T(1,128)}), s32[64,1,8]{2,1,0:T(1,128)S(1)}, u32[]{:S(2)}, u32[]{:S(2)}) async-start(s32[64,1,8]{2,1,0:T(1,128)} %bitcast.6), calls=%async_computation | async-start | bytes 65536 | tf_op jit(solution)/shard_map/all_to_all | solution.py:75
  38.4 15.9 %all-gather.4.cloned.1.call-done = bf16[256,16,128]{0,1,2:T(8,128)(2,1)} async-done(((bf16[256,16,32]{0,1,2:T(8,128)(2,1)}), bf16[256,16,128]{0,1,2:T(8,128)(2,1)}) %all-gather.4.cloned.1.call-update) | async-done | bytes 1048592 | tf_op jit(solution)/shard_map/all_gather | solution.py:50
  54.3 3.2 %copy.75 = bf16[256,16,128]{2,1,0:T(8,128)(2,1)} copy(bf16[256,16,128]{0,1,2:T(8,128)(2,1)} %all-gather.4.cloned.1.call-done) | data formatting | bytes 2097152 | tf_op jit(solution)/shard_map/all_gather | solution.py:50
  57.5 2.1 gather_fusion.1
  59.5 2.6 fusion.35
  62.1 2.5 copy.76
  64.6 3.4 %fusion.29 = f32[64,16,8,32]{3,2,1,0:T(8,128)} fusion(f32[256,16,32]{0,2,1:T(8,128)S(1)} %copy.76, s32[256]{0:T(256)S(1)} %multiply_add_fusion.1, s32[64,8]{1,0:T(8,128)S(1)} %multiply_add_fusion), kind=kOutput, calls=%fused_computation.52 | convolution fusion | flops 805437440 | bytes 1575936 | tf_op jit(solution)/shard_map/dot_general | solution.py:64
  67.9 4.7 %reshape.169 = f32[64,1,4096]{2,1,0:T(1,128)} reshape(f32[64,16,8,32]{3,2,1,0:T(8,128)} %fusion.29) | data formatting | bytes 2097152
  72.6 10.5 %all-to-all-start.1 = ((f32[64,1,4096]{2,1,0:T(1,128)}), f32[64,1,4096]{2,1,0:T(1,128)S(1)}, u32[]{:S(2)}, u32[]{:S(2)}) async-start(f32[64,1,4096]{2,1,0:T(1,128)} %reshape.169), calls=%async_computation.1 | async-start | bytes 2097152 | tf_op jit(solution)/shard_map/all_to_all | solution.py:74
  84.9 27.1 %all-to-all-done.1 = f32[64,1,4096]{2,1,0:T(1,128)S(1)} async-done(((f32[64,1,4096]{2,1,0:T(1,128)}), f32[64,1,4096]{2,1,0:T(1,128)S(1)}, u32[]{:S(2)}, u32[]{:S(2)}) %all-to-all-start.1) | async-done | bytes 1048608 | tf_op jit(solution)/shard_map/all_to_all | solution.py:74
  112.4 3.3 %reduce.6 = f32[64,4096]{1,0:T(8,128)S(1)} reduce(f32[64,1,4096]{2,1,0:T(1,128)S(1)} %all-to-all-done.1, f32[]{:T(128)} %broadcast.92), dimensions={1}, to_apply=%all_to_all.16.reduce_sub_computation | reduce | bytes 2097156 | tf_op jit(solution)/shard_map/all_to_all | solution.py:74
  115.7 2.7 %reshape.170 = f32[64,16,8,32]{3,2,1,0:T(8,128)} reshape(f32[64,4096]{1,0:T(8,128)S(1)} %reduce.6) | data formatting | bytes 2097152
  118.4 5.1 %copy.77 = f32[64,8,16,32]{3,2,1,0:T(8,128)} copy(f32[64,8,16,32]{3,1,2,0:T(8,128)} %bitcast.105) | data formatting | bytes 2097152 | tf_op jit(solution)/shard_map/all_to_all | solution.py:74
  123.5 3.5 %reshape_reshape.3 = f32[512,512]{1,0:T(8,128)S(1)} reshape(f32[64,8,16,32]{3,2,1,0:T(8,128)} %copy.77) | data formatting | bytes 2097152 | tf_op jit(solution)/shard_map/reshape;reshape | solution.py:11
  129.5 13.3 %all_gather.13 = bf16[32,16,128]{0,1,2:T(8,128)(2,1)S(1)} all-gather(bf16[32,16,32]{0,1,2:T(8,128)(2,1)S(1)} %copy.79), channel_id=1, replica_groups=mesh['sub'=64,'harm'=4] {'harm'}, dimensions={2}, use_global_device_ids=true | all-gather | bytes 163840 | tf_op jit(solution)/shard_map/all_gather | solution.py:81
  143.6 2.8 %gather_fusion.2 = bf16[512,16,32]{2,1,0:T(8,128)(2,1)} fusion(bf16[32,16,32]{2,1,0:T(8,128)(2,1)S(1)} %get-tuple-element.12, s32[1024]{0:T(1024)S(1)} %pad_clamp_fusion), kind=kCustom, calls=%fused_computation.2 | custom fusion | bytes 1050624 | tf_op jit(solution)/shard_map/gather | solution.py:86
  146.4 3.7 %reshape.171 = bf16[64,2,2048]{2,1,0:T(2,128)(2,1)S(1)} reshape(bf16[64,8,16,32]{3,2,1,0:T(8,128)(2,1)} %bitcast.107) | data formatting | bytes 1048576
  150.1 22.9 %all_to_all.22 = bf16[64,2,2048]{2,1,0:T(2,128)(2,1)S(1)} all-to-all(bf16[64,2,2048]{2,1,0:T(2,128)(2,1)S(1)} %reshape.171), channel_id=1, replica_groups=mesh['sub'=64,'harm'=4] {'sub'}, dimensions={0} | all-to-all | bytes 1048576 | tf_op jit(solution)/shard_map/all_to_all | solution.py:87
  174.0 2.1 reshape.114
  177.5 21.9 %all-gather.6.cloned.1.call-done = bf16[256,16,128]{0,1,2:T(8,128)(2,1)} async-done(((bf16[256,16,32]{0,1,2:T(8,128)(2,1)}), bf16[256,16,128]{0,1,2:T(8,128)(2,1)}) %all-gather.6.cloned.1.call-update) | async-done | bytes 1048592 | tf_op jit(solution)/shard_map/all_gather | solution.py:93
  199.4 2.5 copy.83
  201.9 2.8 %fusion.36 = f32[256,16,32]{2,1,0:T(8,128)S(1)} fusion(bf16[256,16,128]{2,1,0:T(8,128)(2,1)S(1)} %copy.83, bf16[256,32,128]{2,1,0:T(8,128)(2,1)} %param.17), kind=kOutput, calls=%fused_computation.55 | convolution fusion | flops 33554432 | bytes 3670016 | tf_op jit(solution)/shard_map/tok,trk->tro/dot_general | solution.py:19
  208.9 26.3 %all-gather.8.cloned.1.call-done = bf16[256,16,128]{0,1,2:T(8,128)(2,1)} async-done(((bf16[256,16,32]{0,1,2:T(8,128)(2,1)}), bf16[256,16,128]{0,1,2:T(8,128)(2,1)}) %all-gather.8.cloned.1.call-update) | async-done | bytes 1048592 | tf_op jit(solution)/shard_map/all_gather | solution.py:96
  235.2 2.5 copy.86
  237.7 2.7 %gather_fusion.3 = bf16[512,16,128]{2,1,0:T(8,128)(2,1)} fusion(bf16[256,16,128]{2,1,0:T(8,128)(2,1)S(1)} %copy.86, s32[1024]{0:T(1024)S(1)} %pad_clamp_fusion.2), kind=kCustom, calls=%fused_computation.3 | custom fusion | bytes 4196352 | tf_op jit(solution)/shard_map/gather | solution.py:97
  240.4 7.1 %fusion.37 = f32[512,16,32]{2,1,0:T(8,128)} fusion(bf16[512,16,128]{2,1,0:T(8,128)(2,1)} %gather_fusion.3, bf16[512,32,128]{2,1,0:T(8,128)(2,1)} %param.13), kind=kOutput, calls=%fused_computation.56 | convolution fusion | flops 67108864 | bytes 7340032 | tf_op jit(solution)/shard_map/tok,trk->tro/dot_general | solution.py:19
  247.5 2.9 %copy.87 = f32[512,16,32]{0,2,1:T(8,128)S(1)} copy(f32[512,16,32]{2,1,0:T(8,128)} %fusion.37) | data formatting | bytes 2097152 | tf_op jit(solution)/shard_map/tok,trk->tro/dot_general | solution.py:19
  250.4 1.5 fusion.2
  (59 shorter events, 16.3 us)
Async XLA Ops:
  7.2 52.4 %copy-start = (bf16[256,32,128]{2,1,0:T(8,128)(2,1)S(1)}, bf16[256,32,128]{2,1,0:T(8,128)(2,1)}, u32[]{:S(2)}) copy-start(bf16[256,32,128]{2,1,0:T(8,128)(2,1)} %param.16) | copy-start | bytes 6291460
  7.2 47.1 %all-gather.4.cloned.1.call-start = ((), (), s32[]{:S(2)}) async-start(), calls=%async_computation.3 | async-start | bytes 1310720 | tf_op jit(solution)/shard_map/all_gather | solution.py:50
  20.1 2.8 %copy-start.5 = (s32[512]{0:T(512)S(1)}, s32[512]{0:T(512)}, u32[]{:S(2)}) copy-start(s32[512]{0:T(512)} %param.14) | copy-start | bytes 6148
  22.9 1.6 copy-start.4
  22.9 2.6 copy-start.7
  22.9 15.5 %copy-start.6 = (s32[256]{0:T(256)S(1)}, s32[256]{0:T(256)}, u32[]{:S(2)}) copy-start(s32[256]{0:T(256)} %param.18) | copy-start | bytes 3076
  26.4 46.3 %all-to-all-start = ((s32[64,1,8]{2,1,0:T(1,128)}), s32[64,1,8]{2,1,0:T(1,128)S(1)}, u32[]{:S(2)}, u32[]{:S(2)}) async-start(s32[64,1,8]{2,1,0:T(1,128)} %bitcast.6), calls=%async_computation | async-start | bytes 65536 | tf_op jit(solution)/shard_map/all_to_all | solution.py:75
  72.6 39.3 %all-to-all-start.1 = ((f32[64,1,4096]{2,1,0:T(1,128)}), f32[64,1,4096]{2,1,0:T(1,128)S(1)}, u32[]{:S(2)}, u32[]{:S(2)}) async-start(f32[64,1,4096]{2,1,0:T(1,128)} %reshape.169), calls=%async_computation.1 | async-start | bytes 2097152 | tf_op jit(solution)/shard_map/all_to_all | solution.py:74
  83.2 116.2 %all-gather.6.cloned.1.call-start = ((), (), s32[]{:S(2)}) async-start(), calls=%async_computation.4 | async-start | bytes 1310720 | tf_op jit(solution)/shard_map/all_gather | solution.py:93
  127.0 1.0 copy-start.3
  127.1 16.3 %copy-start.2 = (bf16[32,32,128]{2,1,0:T(8,128)(2,1)S(1)}, bf16[32,32,128]{2,1,0:T(8,128)(2,1)}, u32[]{:S(2)}) copy-start(bf16[32,32,128]{2,1,0:T(8,128)(2,1)} %param.21) | copy-start | bytes 786436
  177.5 57.8 %all-gather.8.cloned.1.call-start = ((), (), s32[]{:S(2)}) async-start(), calls=%async_computation.5 | async-start | bytes 1310720 | tf_op jit(solution)/shard_map/all_gather | solution.py:96
  247.5 4.4 %copy-start.1 = (bf16[256,32,128]{2,1,0:T(8,128)(2,1)S(1)}, bf16[256,32,128]{2,1,0:T(8,128)(2,1)}, u32[]{:S(2)}) copy-start(bf16[256,32,128]{2,1,0:T(8,128)(2,1)} %param.16) | copy-start | bytes 6291460
Sparse Core Ops, SparseCore 0:
  24.6 29.6 all-gather.3
  177.6 21.7 all-gather.5
  208.2 27.0 all-gather.7
where the time goes:
time: 259 us; the launch traced here: 258 us
  waiting for transfers between devices  91.2 us (35%)
  local copies, waits for them, and re-layouts  60 us (23%)
  blocking collectives  36.2 us (14%)
  matrix products  28.3 us (11%)
  starting transfers between devices  22.9 us (9%)
  between operations  14.1 us (5%)
  other arithmetic  5.77 us (2%)
    all_to_all x1, waiting for transfers between devices, on_device(): lax.all_to_all(send_values, 'sub', split_axis=0, concat_axis=0, tiled=True)  27.1 us
    all_gather x1, waiting for transfers between devices, on_device(): update_full = lax.all_gather(update_low, 'harm', axis=2, tiled=True)  26.3 us
    all_to_all x1, blocking collectives, on_device(): lax.all_to_all(replies, 'sub', split_axis=0, concat_axis=0, tiled=True)  22.9 us
    all_gather x1, waiting for transfers between devices, on_device(): touch_full = lax.all_gather(touch_low, 'harm', axis=2, tiled=True)  21.9 us
    dot_general x3, matrix products, tile_product(): jnp.einsum('tok,trk->tro', tile_set, columns, preferred_element_type=jnp....  16.9 us
    unnamed x22, local copies, waits for them, and re-layouts  15.9 us
    all_gather x1, waiting for transfers between devices, on_device(): first_full = lax.all_gather(first_pass, 'harm', axis=2, tiled=True)  15.9 us
    all_gather x1, blocking collectives, on_device(): residual_full = lax.all_gather(residual_low, 'harm', axis=2, tiled=True)  13.3 us
  transfers between devices with their start and end apart: 5, of which 4 were waited for; matrix products, arithmetic and copies ran while one was open for 8% of the time, Pallas kernels for 0%

commit v1 on v0

--- a/solution.py
+++ b/solution.py
@@ -78,7 +78,18 @@
         arrived.reshape((sub_count * capacity,) + value_shape), arrived_rows.reshape(-1), row_count
     )
     residual_low = (own_border - incoming).astype(jnp.bfloat16)
-    residual_full = lax.all_gather(residual_low, "harm", axis=2, tiled=True)
+    ways = lax.axis_size("harm")
+    up = [(d, (d + 1) % ways) for d in range(ways)]
+    down = [(d, (d - 1) % ways) for d in range(ways)]
+    earlier_2, later = ([residual_low], [residual_low])
+    for _ in range(ways // 2):
+        earlier_2.append(lax.ppermute(earlier_2[-1], "harm", up))
+    for _ in range((ways - 1) // 2):
+        later.append(lax.ppermute(later[-1], "harm", down))
+    line = jnp.concatenate([*earlier_2[::-1], *later[1:]], axis=2)
+    residual_full = jnp.roll(
+        line, (lax.axis_index("harm") - ways // 2) * residual_low.shape[2], axis=2
+    )
     solved = jnp.einsum(
         "bok,brk->bro", border_inverse, residual_full, preferred_element_type=jnp.float32
     )

time: 259 us -> 257 us (level)
  blocking collectives: 36.2 us -> 23.3 us
  waiting for transfers between devices: 91.2 us -> 99.3 us
  starting transfers between devices: 22.9 us -> 26.2 us
    all_gather x1 -> x0, blocking collectives: 13.3 us -> none  [on_device(): residual_full = lax.all_gather(residual_low, 'harm', axis=2, tiled=True)]
    ppermute x0 -> x3, waiting for transfers between devices: none -> 8.93 us  [the longest x2 8.92 us: on_device(): earlier_2.append(lax.ppermute(earlier_2[-1], 'harm', up))]
    ppermute x0 -> x3, starting transfers between devices: none -> 3.39 us  [the longest x1 3 us: on_device(): later.append(lax.ppermute(later[-1], 'harm', down))]
    unnamed x22 -> x24, local copies, waits for them, and re-layouts: 15.9 us -> 16 us
  transfers between devices with their start and end apart: 5 -> 8, of which waited for: 4 -> 6; matrix products, arithmetic and copies ran while one was open for 8% -> 8% of each run, Pallas kernels for 0% -> 0%
where the time goes in v1:
time: 257 us; the launch traced here: 256 us
  waiting for transfers between devices  99.3 us (39%)
  local copies, waits for them, and re-layouts  60.1 us (23%)
  matrix products  28.3 us (11%)
  starting transfers between devices  26.2 us (10%)
  blocking collectives  23.3 us (9%)
  between operations  14.1 us (5%)
  other arithmetic  4.95 us (2%)
    all_to_all x1, waiting for transfers between devices, on_device(): lax.all_to_all(send_values, 'sub', split_axis=0, concat_axis=0, tiled=True)  27.2 us
    all_gather x1, waiting for transfers between devices, on_device(): update_full = lax.all_gather(update_low, 'harm', axis=2, tiled=True)  26.3 us
    all_to_all x1, blocking collectives, on_device(): lax.all_to_all(replies, 'sub', split_axis=0, concat_axis=0, tiled=True)  23.3 us
    all_gather x1, waiting for transfers between devices, on_device(): touch_full = lax.all_gather(touch_low, 'harm', axis=2, tiled=True)  20.9 us
    dot_general x3, matrix products, tile_product(): jnp.einsum('tok,trk->tro', tile_set, columns, preferred_element_type=jnp....  16.9 us
    unnamed x24, local copies, waits for them, and re-layouts  16 us
    all_gather x1, waiting for transfers between devices, on_device(): first_full = lax.all_gather(first_pass, 'harm', axis=2, tiled=True)  15.9 us
    all_to_all x1, starting transfers between devices, on_device(): lax.all_to_all(send_rows, 'sub', split_axis=0, concat_axis=0, tiled=True)  12 us
  transfers between devices with their start and end apart: 8, of which 6 were waited for; matrix products, arithmetic and copies ran while one was open for 8% of the time, Pallas kernels for 0%

profile of v1, /device:TPU:2, one launch (start us, length us, event | category | flops | bytes accessed | tf_op | source)
XLA Modules:
  0.0 256.3 jit_solution(16846532182387009536)
XLA Ops:
  7.2 2.4 copy.70
  9.6 2.7 %gather_fusion = bf16[512,16,128]{2,1,0:T(8,128)(2,1)} fusion(bf16[256,16,128]{2,1,0:T(8,128)(2,1)S(1)} %bitcast.105, s32[1024]{0:T(1024)S(1)} %pad_clamp_fusion.2), kind=kCustom, calls=%fused_computation | custom fusion | bytes 4196352 | tf_op jit(solution)/shard_map/gather | solution.py:47
  12.4 7.1 %fusion.36 = f32[512,16,32]{2,1,0:T(8,128)} fusion(bf16[512,16,128]{2,1,0:T(8,128)(2,1)} %gather_fusion, bf16[512,32,128]{2,1,0:T(8,128)(2,1)} %param.13), kind=kOutput, calls=%fused_computation.56 | convolution fusion | flops 67108864 | bytes 7340032 | tf_op jit(solution)/shard_map/tok,trk->tro/dot_general | solution.py:19
  19.4 2.8 %copy.71 = f32[512,16,32]{0,2,1:T(8,128)S(1)} copy(f32[512,16,32]{2,1,0:T(8,128)} %fusion.36) | data formatting | bytes 2097152 | tf_op jit(solution)/shard_map/tok,trk->tro/dot_general | solution.py:19
  25.7 12.0 %all-to-all-start = ((s32[64,1,8]{2,1,0:T(1,128)}), s32[64,1,8]{2,1,0:T(1,128)S(1)}, u32[]{:S(2)}, u32[]{:S(2)}) async-start(s32[64,1,8]{2,1,0:T(1,128)} %bitcast.6), calls=%async_computation | async-start | bytes 65536 | tf_op jit(solution)/shard_map/all_to_all | solution.py:75
  37.8 15.9 %all-gather.4.cloned.1.call-done = bf16[256,16,128]{0,1,2:T(8,128)(2,1)} async-done(((bf16[256,16,32]{0,1,2:T(8,128)(2,1)}), bf16[256,16,128]{0,1,2:T(8,128)(2,1)}) %all-gather.4.cloned.1.call-update) | async-done | bytes 1048592 | tf_op jit(solution)/shard_map/all_gather | solution.py:50
  53.6 3.2 %copy.73 = bf16[256,16,128]{2,1,0:T(8,128)(2,1)} copy(bf16[256,16,128]{0,1,2:T(8,128)(2,1)} %all-gather.4.cloned.1.call-done) | data formatting | bytes 2097152 | tf_op jit(solution)/shard_map/all_gather | solution.py:50
  56.8 2.1 gather_fusion.1
  58.9 2.5 fusion.37
  61.4 2.5 copy.74
  63.9 3.4 %fusion.31 = f32[64,16,8,32]{3,2,1,0:T(8,128)} fusion(f32[256,16,32]{0,2,1:T(8,128)S(1)} %copy.74, s32[256]{0:T(256)S(1)} %multiply_add_fusion.1, s32[64,8]{1,0:T(8,128)S(1)} %multiply_add_fusion), kind=kOutput, calls=%fused_computation.55 | convolution fusion | flops 805437440 | bytes 1575936 | tf_op jit(solution)/shard_map/dot_general | solution.py:64
  67.3 4.7 %reshape.169 = f32[64,1,4096]{2,1,0:T(1,128)} reshape(f32[64,16,8,32]{3,2,1,0:T(8,128)} %fusion.31) | data formatting | bytes 2097152
  72.0 10.5 %all-to-all-start.1 = ((f32[64,1,4096]{2,1,0:T(1,128)}), f32[64,1,4096]{2,1,0:T(1,128)S(1)}, u32[]{:S(2)}, u32[]{:S(2)}) async-start(f32[64,1,4096]{2,1,0:T(1,128)} %reshape.169), calls=%async_computation.1 | async-start | bytes 2097152 | tf_op jit(solution)/shard_map/all_to_all | solution.py:74
  84.1 27.2 %all-to-all-done.1 = f32[64,1,4096]{2,1,0:T(1,128)S(1)} async-done(((f32[64,1,4096]{2,1,0:T(1,128)}), f32[64,1,4096]{2,1,0:T(1,128)S(1)}, u32[]{:S(2)}, u32[]{:S(2)}) %all-to-all-start.1) | async-done | bytes 1048608 | tf_op jit(solution)/shard_map/all_to_all | solution.py:74
  111.8 3.3 %reduce.6 = f32[64,4096]{1,0:T(8,128)S(1)} reduce(f32[64,1,4096]{2,1,0:T(1,128)S(1)} %all-to-all-done.1, f32[]{:T(128)} %broadcast.93), dimensions={1}, to_apply=%all_to_all.16.reduce_sub_computation | reduce | bytes 2097156 | tf_op jit(solution)/shard_map/all_to_all | solution.py:74
  115.1 2.7 %reshape.170 = f32[64,16,8,32]{3,2,1,0:T(8,128)} reshape(f32[64,4096]{1,0:T(8,128)S(1)} %reduce.6) | data formatting | bytes 2097152
  117.8 5.1 %copy.75 = f32[64,8,16,32]{3,2,1,0:T(8,128)} copy(f32[64,8,16,32]{3,1,2,0:T(8,128)} %bitcast.104) | data formatting | bytes 2097152 | tf_op jit(solution)/shard_map/all_to_all | solution.py:74
  122.8 3.5 %reshape_reshape.3 = f32[512,512]{1,0:T(8,128)S(1)} reshape(f32[64,8,16,32]{3,2,1,0:T(8,128)} %copy.75) | data formatting | bytes 2097152 | tf_op jit(solution)/shard_map/reshape;reshape | solution.py:11
  129.2 3.0 %collective-permute-start.2 = (bf16[32,16,32]{2,0,1:T(8,128)(2,1)S(1)}, bf16[32,16,32]{2,0,1:T(8,128)(2,1)S(1)}, u32[]{:S(2)}, u32[]{:S(2)}) collective-permute-start(bf16[32,16,32]{2,0,1:T(8,128)(2,1)S(1)} %fusion.1), channel_id=1, source_target_pairs={{0,3},{1,0},{2,1},{3,2},{4,7},{5,4},{6,5},{7,6},{8,11},{9,8},{10,9... | collective-permute-start | bytes 98312 | tf_op jit(solution)/shard_map/ppermute | solution.py:88
  132.2 2.8 %collective-permute-done = bf16[32,16,32]{2,0,1:T(8,128)(2,1)S(1)} collective-permute-done((bf16[32,16,32]{2,0,1:T(8,128)(2,1)S(1)}, bf16[32,16,32]{2,0,1:T(8,128)(2,1)S(1)}, u32[]{:S(2)}, u32[]{:S(2)}) %collective-permute-start) | collective-permute-done | bytes 32800 | tf_op jit(solution)/shard_map/ppermute | solution.py:86
  135.0 6.2 %collective-permute-done.1 = bf16[32,16,32]{2,0,1:T(8,128)(2,1)S(1)} collective-permute-done((bf16[32,16,32]{2,0,1:T(8,128)(2,1)S(1)}, bf16[32,16,32]{2,0,1:T(8,128)(2,1)S(1)}, u32[]{:S(2)}, u32[]{:S(2)}) %collective-permute-start.1) | collective-permute-done | bytes 32800 | tf_op jit(solution)/shard_map/ppermute | solution.py:86
  142.0 2.8 %gather_fusion.2 = bf16[512,16,32]{2,1,0:T(8,128)(2,1)} fusion(bf16[32,16,32]{2,1,0:T(8,128)(2,1)S(1)} %get-tuple-element.12, s32[1024]{0:T(1024)S(1)} %pad_clamp_fusion), kind=kCustom, calls=%fused_computation.2 | custom fusion | bytes 1050624 | tf_op jit(solution)/shard_map/gather | solution.py:97
  144.8 3.7 %reshape.171 = bf16[64,2,2048]{2,1,0:T(2,128)(2,1)S(1)} reshape(bf16[64,8,16,32]{3,2,1,0:T(8,128)(2,1)} %bitcast.106) | data formatting | bytes 1048576
  148.5 23.3 %all_to_all.22 = bf16[64,2,2048]{2,1,0:T(2,128)(2,1)S(1)} all-to-all(bf16[64,2,2048]{2,1,0:T(2,128)(2,1)S(1)} %reshape.171), channel_id=1, replica_groups=mesh['sub'=64,'harm'=4] {'sub'}, dimensions={0} | all-to-all | bytes 1048576 | tf_op jit(solution)/shard_map/all_to_all | solution.py:98
  176.3 20.9 %all-gather.6.cloned.1.call-done = bf16[256,16,128]{0,1,2:T(8,128)(2,1)} async-done(((bf16[256,16,32]{0,1,2:T(8,128)(2,1)}), bf16[256,16,128]{0,1,2:T(8,128)(2,1)}) %all-gather.6.cloned.1.call-update) | async-done | bytes 1048592 | tf_op jit(solution)/shard_map/all_gather | solution.py:104
  197.2 2.5 copy.80
  199.7 2.8 %fusion.38 = f32[256,16,32]{2,1,0:T(8,128)S(1)} fusion(bf16[256,16,128]{2,1,0:T(8,128)(2,1)S(1)} %copy.80, bf16[256,32,128]{2,1,0:T(8,128)(2,1)} %param.17), kind=kOutput, calls=%fused_computation.58 | convolution fusion | flops 33554432 | bytes 3670016 | tf_op jit(solution)/shard_map/tok,trk->tro/dot_general | solution.py:19
  206.7 26.3 %all-gather.8.cloned.1.call-done = bf16[256,16,128]{0,1,2:T(8,128)(2,1)} async-done(((bf16[256,16,32]{0,1,2:T(8,128)(2,1)}), bf16[256,16,128]{0,1,2:T(8,128)(2,1)}) %all-gather.8.cloned.1.call-update) | async-done | bytes 1048592 | tf_op jit(solution)/shard_map/all_gather | solution.py:107
  233.1 2.5 copy.83
  235.5 2.7 %gather_fusion.3 = bf16[512,16,128]{2,1,0:T(8,128)(2,1)} fusion(bf16[256,16,128]{2,1,0:T(8,128)(2,1)S(1)} %copy.83, s32[1024]{0:T(1024)S(1)} %pad_clamp_fusion.2), kind=kCustom, calls=%fused_computation.3 | custom fusion | bytes 4196352 | tf_op jit(solution)/shard_map/gather | solution.py:108
  238.3 7.1 %fusion.39 = f32[512,16,32]{2,1,0:T(8,128)} fusion(bf16[512,16,128]{2,1,0:T(8,128)(2,1)} %gather_fusion.3, bf16[512,32,128]{2,1,0:T(8,128)(2,1)} %param.13), kind=kOutput, calls=%fused_computation.59 | convolution fusion | flops 67108864 | bytes 7340032 | tf_op jit(solution)/shard_map/tok,trk->tro/dot_general | solution.py:19
  245.3 2.9 %copy.84 = f32[512,16,32]{0,2,1:T(8,128)S(1)} copy(f32[512,16,32]{2,1,0:T(8,128)} %fusion.39) | data formatting | bytes 2097152 | tf_op jit(solution)/shard_map/tok,trk->tro/dot_general | solution.py:19
  (66 shorter events, 19.3 us)
Async XLA Ops:
  7.2 51.7 %copy-start = (bf16[256,32,128]{2,1,0:T(8,128)(2,1)S(1)}, bf16[256,32,128]{2,1,0:T(8,128)(2,1)}, u32[]{:S(2)}) copy-start(bf16[256,32,128]{2,1,0:T(8,128)(2,1)} %param.16) | copy-start | bytes 6291460
  7.2 2.4 copy-start.7
  7.2 46.4 %all-gather.4.cloned.1.call-start = ((), (), s32[]{:S(2)}) async-start(), calls=%async_computation.3 | async-start | bytes 1310720 | tf_op jit(solution)/shard_map/all_gather | solution.py:50
  19.4 2.8 %copy-start.5 = (s32[512]{0:T(512)S(1)}, s32[512]{0:T(512)}, u32[]{:S(2)}) copy-start(s32[512]{0:T(512)} %param.14) | copy-start | bytes 6148
  22.2 1.6 copy-start.4
  22.3 2.6 %copy-start.8 = (s32[256]{0:T(256)S(1)}, s32[256]{0:T(256)}, u32[]{:S(2)}) copy-start(s32[256]{0:T(256)} %param.20) | copy-start | bytes 3076
  22.3 15.5 %copy-start.6 = (s32[256]{0:T(256)S(1)}, s32[256]{0:T(256)}, u32[]{:S(2)}) copy-start(s32[256]{0:T(256)} %param.18) | copy-start | bytes 3076
  25.7 46.3 %all-to-all-start = ((s32[64,1,8]{2,1,0:T(1,128)}), s32[64,1,8]{2,1,0:T(1,128)S(1)}, u32[]{:S(2)}, u32[]{:S(2)}) async-start(s32[64,1,8]{2,1,0:T(1,128)} %bitcast.6), calls=%async_computation | async-start | bytes 65536 | tf_op jit(solution)/shard_map/all_to_all | solution.py:75
  72.0 39.3 %all-to-all-start.1 = ((f32[64,1,4096]{2,1,0:T(1,128)}), f32[64,1,4096]{2,1,0:T(1,128)S(1)}, u32[]{:S(2)}, u32[]{:S(2)}) async-start(f32[64,1,4096]{2,1,0:T(1,128)} %reshape.169), calls=%async_computation.1 | async-start | bytes 2097152 | tf_op jit(solution)/shard_map/all_to_all | solution.py:74
  82.5 114.7 %all-gather.6.cloned.1.call-start = ((), (), s32[]{:S(2)}) async-start(), calls=%async_computation.4 | async-start | bytes 1310720 | tf_op jit(solution)/shard_map/all_gather | solution.py:104
  126.4 1.0 copy-start.3
  126.4 15.3 %copy-start.2 = (bf16[32,32,128]{2,1,0:T(8,128)(2,1)S(1)}, bf16[32,32,128]{2,1,0:T(8,128)(2,1)}, u32[]{:S(2)}) copy-start(bf16[32,32,128]{2,1,0:T(8,128)(2,1)} %param.21) | copy-start | bytes 786436
  128.7 6.3 %collective-permute-start = (bf16[32,16,32]{2,0,1:T(8,128)(2,1)S(1)}, bf16[32,16,32]{2,0,1:T(8,128)(2,1)S(1)}, u32[]{:S(2)}, u32[]{:S(2)}) collective-permute-start(bf16[32,16,32]{2,0,1:T(8,128)(2,1)S(1)} %fusion.1), channel_id=1, source_target_pairs={{0,1},{1,2},{2,3},{3,0},{4,5},{5,6},{6,7},{7,4},{8,9},{9,10},{10,1... | collective-permute-start | bytes 98312 | tf_op jit(solution)/shard_map/ppermute | solution.py:86
  129.2 5.8 %collective-permute-start.2 = (bf16[32,16,32]{2,0,1:T(8,128)(2,1)S(1)}, bf16[32,16,32]{2,0,1:T(8,128)(2,1)S(1)}, u32[]{:S(2)}, u32[]{:S(2)}) collective-permute-start(bf16[32,16,32]{2,0,1:T(8,128)(2,1)S(1)} %fusion.1), channel_id=1, source_target_pairs={{0,3},{1,0},{2,1},{3,2},{4,7},{5,4},{6,5},{7,6},{8,11},{9,8},{10,9... | collective-permute-start | bytes 98312 | tf_op jit(solution)/shard_map/ppermute | solution.py:88
  134.9 6.2 %collective-permute-start.1 = (bf16[32,16,32]{2,0,1:T(8,128)(2,1)S(1)}, bf16[32,16,32]{2,0,1:T(8,128)(2,1)S(1)}, u32[]{:S(2)}, u32[]{:S(2)}) collective-permute-start(bf16[32,16,32]{2,0,1:T(8,128)(2,1)S(1)} %collective-permute-done), channel_id=1, source_target_pairs={{0,1},{1,2},{2,3},{3,0},{4,5},{5,6},{6,7},{7,4},{8,9},{9,10},{10,1... | collective-permute-start | bytes 98312 | tf_op jit(solution)/shard_map/ppermute | solution.py:86
  176.3 56.8 %all-gather.8.cloned.1.call-start = ((), (), s32[]{:S(2)}) async-start(), calls=%async_computation.5 | async-start | bytes 1310720 | tf_op jit(solution)/shard_map/all_gather | solution.py:107
  245.3 4.4 %copy-start.1 = (bf16[256,32,128]{2,1,0:T(8,128)(2,1)S(1)}, bf16[256,32,128]{2,1,0:T(8,128)(2,1)}, u32[]{:S(2)}) copy-start(bf16[256,32,128]{2,1,0:T(8,128)(2,1)} %param.16) | copy-start | bytes 6291460
Sparse Core Ops, SparseCore 0:
  24.0 29.6 all-gather.3
  176.4 20.8 all-gather.5
  206.0 27.0 all-gather.7
